TPU v7x, 256 devices: a whole 4x4x8 slice. The times are simulated.
256 devices in a mesh: ctx: 4 (over y), exp: 64 (over z, x, core).
Axes of the slice: x: 4, y: 4, z: 8, core: 2. Of those that a mesh axis runs over, the one named last changes fastest.
Arguments:
- residual_in: bfloat16 [64, 256, 1536], P('exp', 'ctx'), may hold values from -6 to 6
- queries: bfloat16 [64, 256, 1536], P('exp', 'ctx'), may hold values from -6 to 6
- new_kv: bfloat16 [64, 256, 1024], P('exp', 'ctx'), may hold values from -6 to 6
- cache_kv: bfloat16 [64, 4096, 1024], P('exp', 'ctx'), may hold values from -6 to 6
- cache_len: int32 [64], P('exp'), may hold values from 1 to 4096, 133120 in all
- out_proj: bfloat16 [1536, 1536], replicated, may hold values from -0.625 to 0.625
- norm_gain: float32 [1536], replicated, may hold values from 0.1 to 1.9
- routes: int32 [64, 256, 6], P('exp', 'ctx'), may hold values from 0 to 63, all different within a row; in each aligned block of 64 rows (0 to 63, 64 to 127, ..., all dimensions but the last counted through in order) at most 9 rows name the same one
- route_w: bfloat16 [64, 256, 6], P('exp', 'ctx'), may hold values from 0.049804688 to 0.5
- w_gate_up: bfloat16 [64, 1536, 1024], P('exp'), may hold values from -0.15625 to 0.15625
- w_down: bfloat16 [64, 512, 1536], P('exp'), may hold values from -0.25 to 0.25
Outputs:
- layer_out: bfloat16 [64, 256, 1536], P('exp', 'ctx')
Inputs may be any that keep to these rules, and one draw needn't show every extreme that they name: `cache_len`: the largest length is exactly 4096. `routes`: each token names 6 different experts; among the new tokens of one device (aligned blocks of 64 tokens) no expert is named by more than 9 tokens, a bound that some block reaches.
All inputs are finite; a program needn't handle non-finite values. No bound on the sum of `cache_len` on one device may be relied on, other than what follows from the above.
Results may differ from a plain program's by a relative error of at most 0.02.
Values may be sent and summed in bfloat16 or wider, within the bound.
No kernel may reach another device: no remote copies, remote signals or barrier semaphores. Data moves between devices by JAX's collectives and lax.ppermute only.
A program may use at most 128 MiB of HBM per device.

v0:
```python
import jax
import jax.numpy as jnp
from jax import lax
from jax.sharding import PartitionSpec as P

D = 1536
KVH = 4
HD = 128
GROUP = 3
NEG_BIG = -1e30


def local(
    residual_in,
    queries,
    new_kv,
    cache_kv,
    cache_len,
    out_proj,
    norm_gain,
    routes,
    route_w,
    w_gate_up,
    w_down,
):
    tok_count = residual_in.shape[1]
    cache_rows = cache_kv.shape[1]
    n_ctx = lax.axis_size("ctx")
    ctx_pos = lax.axis_index("ctx")
    length = cache_len[0]
    score_scale = HD ** (-0.5)
    heads = KVH * GROUP
    all_queries = lax.all_gather(queries[0], "ctx", axis=0, tiled=True)
    query_total = all_queries.shape[0]
    query_grid = all_queries.reshape(query_total, KVH, GROUP, HD)
    local_keys = jnp.concatenate([cache_kv[0], new_kv[0]], 0)
    key_rows = local_keys.shape[0]
    key_width = local_keys.shape[1] // 2
    key_part = local_keys[:, :key_width].reshape(key_rows, KVH, HD)
    value_part = local_keys[:, key_width:].reshape(key_rows, KVH, HD)
    scores = (
        jnp.einsum("qkgd,rkd->kgqr", query_grid, key_part, preferred_element_type=jnp.float32)
        * score_scale
    )
    row_index = jnp.arange(key_rows)
    cached = row_index < cache_rows
    cache_pos = ctx_pos * cache_rows + row_index
    new_pos = ctx_pos * tok_count + row_index - cache_rows
    query_pos = jnp.arange(query_total)
    usable = jnp.where(
        cached[None, :], (cache_pos < length)[None, :], new_pos[None, :] <= query_pos[:, None]
    )
    part_max = jnp.max(jnp.where(usable, scores, NEG_BIG), -1)
    softmax_terms = jnp.where(usable, jnp.exp(scores - part_max[..., None]), 0.0)
    part_sum = jnp.sum(softmax_terms, -1)
    part_acc = jnp.einsum(
        "kgqr,rkd->qkgd",
        softmax_terms.astype(jnp.bfloat16),
        value_part,
        preferred_element_type=jnp.float32,
    )
    part_acc = part_acc.reshape(n_ctx, tok_count, heads, HD)
    stats = jnp.stack([part_max, part_sum], 0).reshape(2, heads, n_ctx, tok_count)
    stats = stats.transpose(2, 3, 1, 0).reshape(n_ctx, tok_count, heads * 2)
    got_acc = lax.all_to_all(part_acc, "ctx", split_axis=0, concat_axis=0, tiled=True)
    got_stats = lax.all_to_all(stats, "ctx", split_axis=0, concat_axis=0, tiled=True)
    got_stats = got_stats.reshape(n_ctx, tok_count, heads, 2)
    got_max = got_stats[..., 0]
    got_sum = got_stats[..., 1]
    top_max = jnp.max(got_max, 0)
    rescale = jnp.exp(got_max - top_max[None])
    total_sum = jnp.sum(rescale * got_sum, 0)
    total_acc = jnp.sum(rescale[..., None] * got_acc, 0)
    attended = (total_acc / total_sum[..., None]).reshape(tok_count, heads * HD)
    attended = attended.astype(jnp.bfloat16)
    mixed = (
        residual_in[0].astype(jnp.float32)
        + jnp.dot(attended, out_proj, preferred_element_type=jnp.float32)
    ).astype(jnp.bfloat16)
    widened = mixed.astype(jnp.float32)
    normed = (
        widened * lax.rsqrt(jnp.mean(widened * widened, -1, keepdims=True) + 1e-06) * norm_gain
    ).astype(jnp.bfloat16)
    top_count = routes.shape[2]
    local_experts = w_gate_up.shape[0]
    expert_total = local_experts * lax.axis_size("exp")
    capacity = min(tok_count, 3 * tok_count * top_count // (2 * expert_total))
    expert_ids = routes[0].reshape(-1)
    one_hot = (expert_ids[:, None] == jnp.arange(expert_total)[None, :]).astype(jnp.int32)
    before = jnp.cumsum(one_hot, 0) - one_hot
    slot_index = jnp.sum(before * one_hot, 1)
    dest = (expert_ids * capacity + slot_index).reshape(tok_count, top_count)
    slot_ids = jnp.arange(expert_total * capacity)
    hits = dest[None, :, :] == slot_ids[:, None, None]
    select = jnp.any(hits, -1).astype(jnp.bfloat16)
    outgoing = jnp.dot(select, normed, preferred_element_type=jnp.float32).astype(jnp.bfloat16)
    outgoing = outgoing.reshape(expert_total, capacity, D)
    hidden_half = w_gate_up.shape[2] // 2
    incoming = lax.all_to_all(outgoing, "exp", split_axis=0, concat_axis=0, tiled=True)
    item_count = incoming.shape[1]
    grouped = incoming.reshape(-1, local_experts, item_count, incoming.shape[2])
    gate_up = jnp.einsum("sekd,edf->sekf", grouped, w_gate_up, preferred_element_type=jnp.float32)
    activated = (jax.nn.silu(gate_up[..., :hidden_half]) * gate_up[..., hidden_half:]).astype(
        jnp.bfloat16
    )
    result = jnp.einsum(
        "sekf,efd->sekd", activated, w_down, preferred_element_type=jnp.float32
    ).astype(jnp.bfloat16)
    returned = lax.all_to_all(
        result.reshape(incoming.shape), "exp", split_axis=0, concat_axis=0, tiled=True
    )
    weights = route_w[0]
    combine = jnp.sum(
        jnp.where(hits.transpose(1, 0, 2), weights[:, None, :], jnp.zeros((), weights.dtype)), -1
    )
    blended = jnp.dot(combine, returned.reshape(-1, D), preferred_element_type=jnp.float32)
    return (widened + blended).astype(jnp.bfloat16)[None]


def solution(mesh):
    return jax.shard_map(
        local,
        mesh=mesh,
        in_specs=(
            P("exp", "ctx", None),
            P("exp", "ctx", None),
            P("exp", "ctx", None),
            P("exp", "ctx", None),
            P("exp"),
            P(),
            P(),
            P("exp", "ctx", None),
            P("exp", "ctx", None),
            P("exp", None, None),
            P("exp", None, None),
        ),
        out_specs=P("exp", "ctx", None),
        check_vma=False,
    )
```

profile of v0, /device:TPU:2, one launch (start us, length us, event | category | flops | bytes accessed | tf_op | source)
XLA Modules:
  0.0 276.0 jit_solution(6451135125738383920)
XLA Ops:
  0.8 3.2 %fusion.25 = (bf16[1088,512]{1,0:T(8,128)(2,1)}, bf16[1088,512]{1,0:T(8,128)(2,1)}) fusion(bf16[1024,1024]{1,0:T(8,128)(2,1)} %bitcast.119, bf16[64,1024]{1,0:T(8,128)(2,1)} %bitcast.123), kind=kLoop, calls=%fused_computation.28 | loop fusion | flops 4456448 | bytes 4456448 | tf_op jit(solution)/shard_map/concatenate | solution.py:36
  4.0 2.4 copy.119
  6.4 14.6 %all-gather = bf16[1,256,1536]{2,1,0:T(8,128)(2,1)} all-gather(bf16[1,64,1536]{2,1,0:T(8,128)(2,1)S(1)} %copy-done.1), channel_id=2, replica_groups=mesh['ctx'=4,'exp'=64] {'ctx'}, dimensions={1}, use_global_device_ids=true | all-gather | bytes 983040 | tf_op jit(solution)/shard_map/all_gather | solution.py:33
  21.0 2.3 copy.120
  23.3 0.9 fusion.26
  24.2 8.5 %fusion = (f32[4,3,256]{2,1,0:T(4,128)S(1)}, f32[4,1088,256,3]{2,1,3,0:T(8,128)}) fusion(pred[256,1088]{0,1:T(8,128)(4,1)S(1)} %fusion.26, bf16[1088,4,128,1]{0,2,3,1:T(8,128)(2,1)} %bitcast.117, bf16[256,4,3,128]{0,3,2,1:T(8,128)(2,1)} %bitcast.118), kind=kOutput, calls=%fused_computation.2 | convolution fusion | flops 865661952 | bytes 15560704 | tf_op jit(solution)/shard_map/qkgd,rkd->kgqr/dot_general | solution.py:42
  32.8 7.5 %fusion.4 = f32[4,3,256]{2,1,0:T(4,128)S(1)} fusion(f32[4,1088,256,3]{2,1,3,0:T(8,128)} %get-tuple-element.11, f32[4,3,256]{2,1,0:T(4,128)S(1)} %get-tuple-element.10, pred[256,1088]{0,1:T(8,128)(4,1)S(1)} %fusion.26), kind=kLoop, calls=%fused_computation.6 | loop fusion | flops 13366272 | bytes 13672448 | tf_op jit(solution)/shard_map/reduce_sum | solution.py:55
  40.5 0.7 reshape.117
  41.2 4.4 %all-to-all-start = ((f32[4,1,1536]{2,1,0:T(1,128)}), f32[4,1,1536]{2,1,0:T(1,128)S(1)}, u32[]{:S(2)}, u32[]{:S(2)}) async-start(f32[4,1,1536]{2,1,0:T(1,128)} %reshape.117), calls=%async_computation | async-start | bytes 49152 | tf_op jit(solution)/shard_map/all_to_all | solution.py:66
  45.6 2.4 copy.126
  47.9 9.1 %fusion.21 = f32[256,4,3,128]{0,3,2,1:T(8,128)} fusion(bf16[1088,4,128,1]{0,2,3,1:T(8,128)(2,1)} %bitcast.120, f32[4,1088,256,3]{2,1,3,0:T(8,128)} %get-tuple-element.11, f32[4,3,256]{2,1,0:T(4,128)S(1)} %get-tuple-element.10, pred[256,1088]{0,1:T(8,128)(4,1)S(1)} %fusion.26), kind=kOutput, calls=%fused_computation.25 | convolution fusion | flops 869007360 | bytes 16347136 | tf_op jit(solution)/shard_map/kgqr,rkd->qkgd/dot_general | solution.py:56
  57.1 3.0 %copy.128 = f32[256,4,3,128]{3,0,2,1:T(8,128)} copy(f32[256,4,3,128]{0,3,2,1:T(8,128)} %fusion.21) | data formatting | bytes 3145728 | tf_op jit(solution)/shard_map/kgqr,rkd->qkgd/transpose | solution.py:56
  60.1 2.8 copy.129
  63.1 4.8 %all-to-all-start.1 = ((f32[4,64,12,128]{3,1,2,0:T(8,128)}), f32[4,64,12,128]{3,1,2,0:T(8,128)}, u32[]{:S(2)}, u32[]{:S(2)}) async-start(f32[4,64,12,128]{3,1,2,0:T(8,128)} %copy.129), calls=%async_computation.1 | async-start | bytes 3145728 | tf_op jit(solution)/shard_map/all_to_all | solution.py:65
  68.1 0.9 reduce-window.6
  69.6 0.8 fusion.28
  70.4 0.5 broadcast.74
  70.9 0.6 reduce.4
  71.8 14.0 %all-to-all-done.1 = f32[4,64,12,128]{3,1,2,0:T(8,128)} async-done(((f32[4,64,12,128]{3,1,2,0:T(8,128)}), f32[4,64,12,128]{3,1,2,0:T(8,128)}, u32[]{:S(2)}, u32[]{:S(2)}) %all-to-all-start.1) | async-done | bytes 1572896 | tf_op jit(solution)/shard_map/all_to_all | solution.py:65
  85.7 1.9 multiply_reduce_fusion
  87.7 3.5 %multiply_reduce_fusion.1 = (f32[64]{0:T(128)S(1)}, f32[64,1536]{1,0:T(8,128)S(1)}) fusion(bf16[1536,1536]{1,0:T(8,128)(2,1)} %param.16, bf16[1,64,1536]{2,1,0:T(8,128)(2,1)} %param.11, f32[64,12,128]{2,0,1:T(8,128)S(1)} %multiply_reduce_fusion, f32[64,12]{0,1:T(8,128)S(1)} %fusion.41), kind=kOutput, calls=%fused_computation.39 | convolution fusion | flops 302776256 | bytes 5704960 | tf_op jit(solution)/shard_map/dot_general | solution.py:78
  91.1 1.9 convolution_convert_fusion
  93.1 4.2 %reshape.104 = bf16[64,9,1536]{2,1,0:T(8,128)(2,1)} reshape(bf16[576,1536]{1,0:T(8,128)(2,1)} %convolution_convert_fusion) | data formatting | bytes 3538944 | tf_op jit(solution)/shard_map/reshape | solution.py:97
  97.2 85.7 %all_to_all.20 = bf16[64,9,1536]{2,1,0:T(8,128)(2,1)S(1)} all-to-all(bf16[64,9,1536]{2,1,0:T(8,128)(2,1)} %reshape.104), channel_id=1, replica_groups=mesh['ctx'=4,'exp'=64] {'exp'}, dimensions={0} | all-to-all | bytes 3538944 | tf_op jit(solution)/shard_map/all_to_all | solution.py:99
  183.0 2.5 fusion.15
  185.5 1.1 convolution_convert_fusion.1
  186.6 2.8 %copy.138 = bf16[64,9,1536]{2,1,0:T(8,128)(2,1)} copy(bf16[64,9,1536]{2,0,1:T(8,128)(2,1)S(1)} %convolution_convert_fusion.1) | data formatting | bytes 3538944 | tf_op jit(solution)/shard_map/convert_element_type | solution.py:108
  189.4 6.0 %all-to-all-start.3 = ((bf16[64,9,1536]{2,1,0:T(8,128)(2,1)}), bf16[64,9,1536]{2,1,0:T(8,128)(2,1)}, u32[]{:S(2)}, u32[]{:S(2)}) async-start(bf16[64,9,1536]{2,1,0:T(8,128)(2,1)} %copy.138), calls=%async_computation.3 | async-start | bytes 6291456 | tf_op jit(solution)/shard_map/all_to_all | solution.py:109
  195.4 0.8 fusion.31
  196.2 72.8 %all-to-all-done.3 = bf16[64,9,1536]{2,1,0:T(8,128)(2,1)} async-done(((bf16[64,9,1536]{2,1,0:T(8,128)(2,1)}), bf16[64,9,1536]{2,1,0:T(8,128)(2,1)}, u32[]{:S(2)}, u32[]{:S(2)}) %all-to-all-start.3) | async-done | bytes 1769504 | tf_op jit(solution)/shard_map/all_to_all | solution.py:109
  269.1 4.2 %reshape.108 = bf16[576,1536]{1,0:T(8,128)(2,1)} reshape(bf16[64,9,1536]{2,1,0:T(8,128)(2,1)} %all-to-all-done.3) | data formatting | bytes 3538944 | tf_op jit(solution)/shard_map/reshape | solution.py:116
  273.3 2.7 fusion.13
  (38 shorter events, 1.5 us)
Async XLA Ops:
  0.0 183.0 %copy-start = (bf16[1,1536,1024]{2,1,0:T(8,128)(2,1)S(1)}, bf16[1,1536,1024]{2,1,0:T(8,128)(2,1)}, u32[]{:S(2)}) copy-start(bf16[1,1536,1024]{2,1,0:T(8,128)(2,1)} %param.20) | copy-start | bytes 9437188
  4.0 2.4 copy-start.1
  41.2 21.9 %all-to-all-start = ((f32[4,1,1536]{2,1,0:T(1,128)}), f32[4,1,1536]{2,1,0:T(1,128)S(1)}, u32[]{:S(2)}, u32[]{:S(2)}) async-start(f32[4,1,1536]{2,1,0:T(1,128)} %reshape.117), calls=%async_computation | async-start | bytes 49152 | tf_op jit(solution)/shard_map/all_to_all | solution.py:66
  60.1 2.8 copy-start.3
  63.1 22.6 %all-to-all-start.1 = ((f32[4,64,12,128]{3,1,2,0:T(8,128)}), f32[4,64,12,128]{3,1,2,0:T(8,128)}, u32[]{:S(2)}, u32[]{:S(2)}) async-start(f32[4,64,12,128]{3,1,2,0:T(8,128)} %copy.129), calls=%async_computation.1 | async-start | bytes 3145728 | tf_op jit(solution)/shard_map/all_to_all | solution.py:65
  87.6 3.5 %copy-start.2 = (pred[576,64]{0,1:T(8,128)(4,1)S(1)}, pred[576,64]{0,1:T(8,128)(4,1)}, u32[]{:S(2)}) copy-start(pred[576,64]{0,1:T(8,128)(4,1)} %fusion.28) | copy-start | bytes 110596
  87.6 3.5 %copy-start.4 = (f32[1536]{0:T(1024)S(1)}, f32[1536]{0:T(1024)}, u32[]{:S(2)}) copy-start(f32[1536]{0:T(1024)} %param.17) | copy-start | bytes 18436
  183.0 2.5 copy-start.6
  189.4 6.0 %copy-start.5 = (bf16[1,64,6]{1,2,0:T(8,128)(2,1)S(1)}, bf16[1,64,6]{1,2,0:T(8,128)(2,1)}, u32[]{:S(2)}) copy-start(bf16[1,64,6]{1,2,0:T(8,128)(2,1)} %param.19) | copy-start | bytes 2308
  189.4 79.6 %all-to-all-start.3 = ((bf16[64,9,1536]{2,1,0:T(8,128)(2,1)}), bf16[64,9,1536]{2,1,0:T(8,128)(2,1)}, u32[]{:S(2)}, u32[]{:S(2)}) async-start(bf16[64,9,1536]{2,1,0:T(8,128)(2,1)} %copy.138), calls=%async_computation.3 | async-start | bytes 6291456 | tf_op jit(solution)/shard_map/all_to_all | solution.py:109
where the time goes:
time: 277 us; the launch traced here: 276 us
  blocking collectives  100 us (36%)
  waiting for transfers between devices  86.8 us (31%)
  matrix products  29.3 us (11%)
  local copies, waits for them, and re-layouts  26.4 us (10%)
  other arithmetic  17 us (6%)
  starting transfers between devices  15.2 us (5%)
    all_to_all x1, blocking collectives, local(): lax.all_to_all(outgoing, 'exp', split_axis=0, concat_axis=0, tiled=True)  85.7 us
    all_to_all x1, waiting for transfers between devices, local(): lax.all_to_all(result.reshape(incoming.shape), 'exp', split_axis=0, conca...  72.8 us
    all_gather x1, blocking collectives, local(): all_queries = lax.all_gather(queries[0], 'ctx', axis=0, tiled=True)  14.6 us
    all_to_all x1, waiting for transfers between devices, local(): lax.all_to_all(part_acc, 'ctx', split_axis=0, concat_axis=0, tiled=True)  14 us
    dot_general x1, matrix products, local(): jnp.einsum('kgqr,rkd->qkgd', softmax_terms.astype(jnp.bfloat16), value_pa...  9.13 us
    dot_general x1, matrix products, local(): jnp.einsum('qkgd,rkd->kgqr', query_grid, key_part, preferred_element_type...  8.52 us
    reduce_sum x1, other arithmetic, local(): part_sum = jnp.sum(softmax_terms, -1)  7.48 us
    all_to_all x1, starting transfers between devices, local(): lax.all_to_all(result.reshape(incoming.shape), 'exp', split_axis=0, conca...  5.97 us
  transfers between devices with their start and end apart: 3, of which 2 were waited for; matrix products, arithmetic and copies ran while one was open for 8% of the time, Pallas kernels for 0%

commit v1 on v0

--- a/solution.py
+++ b/solution.py
@@ -30,7 +30,15 @@
     length = cache_len[0]
     score_scale = HD ** (-0.5)
     heads = KVH * GROUP
-    all_queries = lax.all_gather(queries[0], "ctx", axis=0, tiled=True)
+    all_queries = jnp.concatenate(
+        jax.lax.all_to_all(
+            jnp.stack(jax.lax.axis_size("ctx") * [queries[0]], axis=0),
+            axis_name="ctx",
+            split_axis=0,
+            concat_axis=0,
+        ),
+        axis=0,
+    )
     query_total = all_queries.shape[0]
     query_grid = all_queries.reshape(query_total, KVH, GROUP, HD)
     local_keys = jnp.concatenate([cache_kv[0], new_kv[0]], 0)

time: 277 us -> 274 us (0.989)
  blocking collectives: 100 us -> 85.7 us
  waiting for transfers between devices: 86.8 us -> 91.3 us
  local copies, waits for them, and re-layouts: 26.4 us -> 29.7 us
  starting transfers between devices: 15.2 us -> 18.4 us
    all_gather x1 -> x0, blocking collectives: 14.6 us -> none  [local(): all_queries = lax.all_gather(queries[0], 'ctx', axis=0, tiled=True)]
    another operation x0 -> x2, local copies, waits for them, and re-layouts: none -> 5.59 us  [the longest x1 3.57 us: local(): query_grid = all_queries.reshape(query_total, KVH, GROUP, HD)]
    all_to_all x0 -> x1, starting transfers between devices: none -> 4.46 us  [local(): jax.lax.all_to_all(jnp.stack(jax.lax.axis_size('ctx') * [queries[0]], axi...]
  transfers between devices with their start and end apart: 3 -> 4, of which waited for: 2 -> 3; matrix products, arithmetic and copies ran while one was open for 8% -> 10% of each run, Pallas kernels for 0% -> 0%
where the time goes in v1:
time: 274 us; the launch traced here: 273 us
  waiting for transfers between devices  91.3 us (33%)
  blocking collectives  85.7 us (31%)
  local copies, waits for them, and re-layouts  29.7 us (11%)
  matrix products  29.7 us (11%)
  starting transfers between devices  18.4 us (7%)
  other arithmetic  16.9 us (6%)
    all_to_all x1, blocking collectives, local(): lax.all_to_all(outgoing, 'exp', split_axis=0, concat_axis=0, tiled=True)  85.7 us
    all_to_all x1, waiting for transfers between devices, local(): lax.all_to_all(result.reshape(incoming.shape), 'exp', split_axis=0, conca...  72.8 us
    all_to_all x1, waiting for transfers between devices, local(): lax.all_to_all(part_acc, 'ctx', split_axis=0, concat_axis=0, tiled=True)  15.8 us
    dot_general x1, matrix products, local(): jnp.einsum('kgqr,rkd->qkgd', softmax_terms.astype(jnp.bfloat16), value_pa...  9.14 us
    dot_general x1, matrix products, local(): jnp.einsum('qkgd,rkd->kgqr', query_grid, key_part, preferred_element_type...  8.92 us
    reduce_sum x1, other arithmetic, local(): part_sum = jnp.sum(softmax_terms, -1)  7.48 us
    all_to_all x1, starting transfers between devices, local(): lax.all_to_all(result.reshape(incoming.shape), 'exp', split_axis=0, conca...  5.97 us
  transfers between devices with their start and end apart: 4, of which 3 were waited for; matrix products, arithmetic and copies ran while one was open for 10% of the time, Pallas kernels for 0%

profile of v1, /device:TPU:2, one launch (start us, length us, event | category | flops | bytes accessed | tf_op | source)
XLA Modules:
  0.0 272.6 jit_solution(530043840084113315)
XLA Ops:
  0.0 2.0 stack.12
  2.0 4.5 %all-to-all-start = ((bf16[4,64,1536]{2,1,0:T(8,128)(2,1)}), bf16[4,64,1536]{2,1,0:T(8,128)(2,1)}, u32[]{:S(2)}, u32[]{:S(2)}) async-start(bf16[4,64,1536]{2,1,0:T(8,128)(2,1)} %stack.12), calls=%async_computation | async-start | bytes 1572864 | tf_op jit(solution)/shard_map/all_to_all | solution.py:34
  7.2 3.1 %fusion.25 = (bf16[1088,512]{1,0:T(8,128)(2,1)}, bf16[1088,512]{1,0:T(8,128)(2,1)}) fusion(bf16[1024,1024]{1,0:T(8,128)(2,1)} %bitcast.117, bf16[64,1024]{1,0:T(8,128)(2,1)S(1)} %bitcast.122), kind=kLoop, calls=%fused_computation.28 | loop fusion | flops 4456448 | bytes 4456448 | tf_op jit(solution)/shard_map/concatenate | solution.py:44
  10.3 2.4 copy.114
  12.6 2.4 copy.120
  15.3 0.9 fusion.26
  16.2 2.7 all-to-all-done
  18.9 3.6 %reshape_reshape.3 = bf16[256,4,3,128]{3,2,1,0:T(4,128)(2,1)} reshape(bf16[4,64,1536]{2,1,0:T(8,128)(2,1)} %all-to-all-done) | data formatting | bytes 1572864 | tf_op jit(solution)/shard_map/reshape;reshape | solution.py:43
  22.5 8.9 %fusion = (f32[4,3,256]{2,1,0:T(4,128)S(1)}, f32[4,1088,256,3]{2,1,3,0:T(8,128)}) fusion(pred[256,1088]{0,1:T(8,128)(4,1)S(1)} %fusion.26, bf16[1088,4,128,1]{0,2,3,1:T(8,128)(2,1)} %bitcast.116, bf16[256,4,3,128]{3,2,1,0:T(4,128)(2,1)} %reshape_reshape.3), kind=kOutput, calls=%fused_computation.2 | convolution fusion | flops 865661952 | bytes 15560704 | tf_op jit(solution)/shard_map/qkgd,rkd->kgqr/dot_general | solution.py:50
  31.5 7.5 %fusion.4 = f32[4,3,256]{2,1,0:T(4,128)S(1)} fusion(f32[4,1088,256,3]{2,1,3,0:T(8,128)} %get-tuple-element.11, f32[4,3,256]{2,1,0:T(4,128)S(1)} %get-tuple-element.10, pred[256,1088]{0,1:T(8,128)(4,1)S(1)} %fusion.26), kind=kLoop, calls=%fused_computation.6 | loop fusion | flops 13366272 | bytes 13672448 | tf_op jit(solution)/shard_map/reduce_sum | solution.py:63
  39.1 0.7 reshape.112
  39.8 3.3 %all-to-all-start.1 = ((f32[4,1,1536]{2,1,0:T(1,128)}), f32[4,1,1536]{2,1,0:T(1,128)S(1)}, u32[]{:S(2)}, u32[]{:S(2)}) async-start(f32[4,1,1536]{2,1,0:T(1,128)} %reshape.112), calls=%async_computation.1 | async-start | bytes 49152 | tf_op jit(solution)/shard_map/all_to_all | solution.py:74
  43.1 9.1 %fusion.21 = f32[256,4,3,128]{0,3,2,1:T(8,128)} fusion(bf16[1088,4,128,1]{0,2,3,1:T(8,128)(2,1)} %bitcast.118, f32[4,1088,256,3]{2,1,3,0:T(8,128)} %get-tuple-element.11, f32[4,3,256]{2,1,0:T(4,128)S(1)} %get-tuple-element.10, pred[256,1088]{0,1:T(8,128)(4,1)S(1)} %fusion.26), kind=kOutput, calls=%fused_computation.25 | convolution fusion | flops 869007360 | bytes 16347136 | tf_op jit(solution)/shard_map/kgqr,rkd->qkgd/dot_general | solution.py:64
  52.2 3.0 %copy.122 = f32[256,4,3,128]{3,0,2,1:T(8,128)} copy(f32[256,4,3,128]{0,3,2,1:T(8,128)} %fusion.21) | data formatting | bytes 3145728 | tf_op jit(solution)/shard_map/kgqr,rkd->qkgd/transpose | solution.py:64
  55.2 2.7 %copy.123 = f32[4,64,12,128]{3,1,2,0:T(8,128)} copy(f32[4,64,12,128]{3,1,0,2:T(8,128)} %bitcast.115) | data formatting | bytes 3145728 | tf_op jit(solution)/shard_map/reshape | solution.py:70
  58.0 4.8 %all-to-all-start.2 = ((f32[4,64,12,128]{3,1,2,0:T(8,128)}), f32[4,64,12,128]{3,1,2,0:T(8,128)}, u32[]{:S(2)}, u32[]{:S(2)}) async-start(f32[4,64,12,128]{3,1,2,0:T(8,128)} %copy.123), calls=%async_computation.2 | async-start | bytes 3145728 | tf_op jit(solution)/shard_map/all_to_all | solution.py:73
  62.9 0.9 reduce-window.6
  64.4 0.8 fusion.28
  66.6 15.8 %all-to-all-done.2 = f32[4,64,12,128]{3,1,2,0:T(8,128)} async-done(((f32[4,64,12,128]{3,1,2,0:T(8,128)}), f32[4,64,12,128]{3,1,2,0:T(8,128)}, u32[]{:S(2)}, u32[]{:S(2)}) %all-to-all-start.2) | async-done | bytes 1572896 | tf_op jit(solution)/shard_map/all_to_all | solution.py:73
  82.4 1.9 multiply_reduce_fusion
  84.3 3.5 %multiply_reduce_fusion.1 = (f32[64]{0:T(128)S(1)}, f32[64,1536]{1,0:T(8,128)S(1)}) fusion(bf16[1536,1536]{1,0:T(8,128)(2,1)} %param.16, bf16[1,64,1536]{2,1,0:T(8,128)(2,1)} %param.11, f32[64,12,128]{2,0,1:T(8,128)S(1)} %multiply_reduce_fusion, f32[64,12]{0,1:T(8,128)S(1)} %fusion.43), kind=kOutput, calls=%fused_computation.41 | convolution fusion | flops 302776256 | bytes 5704960 | tf_op jit(solution)/shard_map/dot_general | solution.py:86
  87.8 1.9 convolution_convert_fusion
  89.7 4.2 %reshape.101 = bf16[64,9,1536]{2,1,0:T(8,128)(2,1)} reshape(bf16[576,1536]{1,0:T(8,128)(2,1)} %convolution_convert_fusion) | data formatting | bytes 3538944 | tf_op jit(solution)/shard_map/reshape | solution.py:105
  93.9 85.7 %all_to_all.25 = bf16[64,9,1536]{2,1,0:T(8,128)(2,1)S(1)} all-to-all(bf16[64,9,1536]{2,1,0:T(8,128)(2,1)} %reshape.101), channel_id=1, replica_groups=mesh['ctx'=4,'exp'=64] {'exp'}, dimensions={0} | all-to-all | bytes 3538944 | tf_op jit(solution)/shard_map/all_to_all | solution.py:107
  179.6 2.5 fusion.15
  182.2 1.1 convolution_convert_fusion.1
  183.3 2.8 %copy.132 = bf16[64,9,1536]{2,1,0:T(8,128)(2,1)} copy(bf16[64,9,1536]{2,0,1:T(8,128)(2,1)S(1)} %convolution_convert_fusion.1) | data formatting | bytes 3538944 | tf_op jit(solution)/shard_map/convert_element_type | solution.py:116
  186.1 6.0 %all-to-all-start.4 = ((bf16[64,9,1536]{2,1,0:T(8,128)(2,1)}), bf16[64,9,1536]{2,1,0:T(8,128)(2,1)}, u32[]{:S(2)}, u32[]{:S(2)}) async-start(bf16[64,9,1536]{2,1,0:T(8,128)(2,1)} %copy.132), calls=%async_computation.4 | async-start | bytes 6291456 | tf_op jit(solution)/shard_map/all_to_all | solution.py:117
  192.1 0.8 fusion.33
  192.9 72.8 %all-to-all-done.4 = bf16[64,9,1536]{2,1,0:T(8,128)(2,1)} async-done(((bf16[64,9,1536]{2,1,0:T(8,128)(2,1)}), bf16[64,9,1536]{2,1,0:T(8,128)(2,1)}, u32[]{:S(2)}, u32[]{:S(2)}) %all-to-all-start.4) | async-done | bytes 1769504 | tf_op jit(solution)/shard_map/all_to_all | solution.py:117
  265.7 4.2 %reshape.105 = bf16[576,1536]{1,0:T(8,128)(2,1)} reshape(bf16[64,9,1536]{2,1,0:T(8,128)(2,1)} %all-to-all-done.4) | data formatting | bytes 3538944 | tf_op jit(solution)/shard_map/reshape | solution.py:124
  270.0 2.7 fusion.13
  (40 shorter events, 2.5 us)
Async XLA Ops:
  0.0 179.6 %copy-start = (bf16[1,1536,1024]{2,1,0:T(8,128)(2,1)S(1)}, bf16[1,1536,1024]{2,1,0:T(8,128)(2,1)}, u32[]{:S(2)}) copy-start(bf16[1,1536,1024]{2,1,0:T(8,128)(2,1)} %param.20) | copy-start | bytes 9437188
  0.0 7.1 %copy-start.2 = (bf16[1,64,1024]{2,1,0:T(8,128)(2,1)S(1)}, bf16[1,64,1024]{2,1,0:T(8,128)(2,1)}, u32[]{:S(2)}) copy-start(bf16[1,64,1024]{2,1,0:T(8,128)(2,1)} %param.13) | copy-start | bytes 393220
  2.0 16.9 %all-to-all-start = ((bf16[4,64,1536]{2,1,0:T(8,128)(2,1)}), bf16[4,64,1536]{2,1,0:T(8,128)(2,1)}, u32[]{:S(2)}, u32[]{:S(2)}) async-start(bf16[4,64,1536]{2,1,0:T(8,128)(2,1)} %stack.12), calls=%async_computation | async-start | bytes 1572864 | tf_op jit(solution)/shard_map/all_to_all | solution.py:34
  10.2 4.8 %copy-start.3 = (s32[1,64,6]{1,0,2:T(1,128)S(1)}, s32[1,64,6]{1,0,2:T(1,128)}, u32[]{:S(2)}) copy-start(s32[1,64,6]{1,0,2:T(1,128)} %param.18) | copy-start | bytes 4612
  39.8 18.2 %all-to-all-start.1 = ((f32[4,1,1536]{2,1,0:T(1,128)}), f32[4,1,1536]{2,1,0:T(1,128)S(1)}, u32[]{:S(2)}, u32[]{:S(2)}) async-start(f32[4,1,1536]{2,1,0:T(1,128)} %reshape.112), calls=%async_computation.1 | async-start | bytes 49152 | tf_op jit(solution)/shard_map/all_to_all | solution.py:74
  58.0 24.4 %all-to-all-start.2 = ((f32[4,64,12,128]{3,1,2,0:T(8,128)}), f32[4,64,12,128]{3,1,2,0:T(8,128)}, u32[]{:S(2)}, u32[]{:S(2)}) async-start(f32[4,64,12,128]{3,1,2,0:T(8,128)} %copy.123), calls=%async_computation.2 | async-start | bytes 3145728 | tf_op jit(solution)/shard_map/all_to_all | solution.py:73
  84.3 3.5 %copy-start.1 = (pred[576,64]{0,1:T(8,128)(4,1)S(1)}, pred[576,64]{0,1:T(8,128)(4,1)}, u32[]{:S(2)}) copy-start(pred[576,64]{0,1:T(8,128)(4,1)} %fusion.28) | copy-start | bytes 110596
  84.3 3.5 %copy-start.4 = (f32[1536]{0:T(1024)S(1)}, f32[1536]{0:T(1024)}, u32[]{:S(2)}) copy-start(f32[1536]{0:T(1024)} %param.17) | copy-start | bytes 18436
  179.6 2.5 copy-start.6
  186.1 6.0 %copy-start.5 = (bf16[1,64,6]{1,2,0:T(8,128)(2,1)S(1)}, bf16[1,64,6]{1,2,0:T(8,128)(2,1)}, u32[]{:S(2)}) copy-start(bf16[1,64,6]{1,2,0:T(8,128)(2,1)} %param.19) | copy-start | bytes 2308
  186.1 79.6 %all-to-all-start.4 = ((bf16[64,9,1536]{2,1,0:T(8,128)(2,1)}), bf16[64,9,1536]{2,1,0:T(8,128)(2,1)}, u32[]{:S(2)}, u32[]{:S(2)}) async-start(bf16[64,9,1536]{2,1,0:T(8,128)(2,1)} %copy.132), calls=%async_computation.4 | async-start | bytes 6291456 | tf_op jit(solution)/shard_map/all_to_all | solution.py:117
